TPU v7x, 512 devices: a whole 4x8x8 slice. The times are simulated.
512 devices in a mesh: segment: 16 (over y, z_lo), ctx: 32 (over x, z_hi, core).
Axes of the slice: x: 4, y: 8, z: 8 (z_hi: 4, z_lo: 2; z = z_hi * 2 + z_lo), core: 2. Of those that a mesh axis runs over, the one named last changes fastest.
Arguments:
- perturbed_frame_activation: bfloat16 [2, 256, 1536], P(None, 'ctx'), may hold values from -8 to 8
- inbound_activation: bfloat16 [16, 256, 1536], P('segment', 'ctx'), may hold values from -6 to 6
- section_block_indices: int32 [16], P('segment'), may hold values from 1 to 2, as said below
- tile_arrival_permutation: int32 [2], replicated, may hold values from 0 to 1, each once
- adaptive_shifting: float32 [16, 2, 1536], P('segment'), may hold values from -6 to 6
- adaptive_scaling: float32 [16, 2, 1536], P('segment'), may hold values from -4 to 4
- tier_query_factor: float32 [16, 2, 1536], P('segment'), may hold values from 0.3 to 3
- tier_skip_coefficient: float32 [16, 2, 1536], P('segment'), may hold values from -12 to 12
- earlier_step_lookup_matrix: bfloat16 [16, 2, 2, 256, 1536], P('segment', None, None, 'ctx'), may hold values from -10.5 to 10.5
- earlier_step_content_matrix: bfloat16 [16, 2, 2, 256, 1536], P('segment', None, None, 'ctx'), may hold values from -3 to 3
Outputs:
- section_out: bfloat16 [16, 2, 256, 1536], P('segment', None, 'ctx')
Inputs may be any that keep to these rules, and one draw needn't show every extreme that they name: `section_block_indices`: some segment uses exactly 2 slots and some exactly 1. `tile_arrival_permutation`: each patch once.
All inputs are finite; a program needn't handle non-finite values.
Results may differ from a plain program's by a relative error of at most 0.013.
Values may be sent and summed in bfloat16 or wider, within the bound.
No kernel may reach another device: no remote copies, remote signals or barrier semaphores. Data moves between devices by JAX's collectives and lax.ppermute only.
A program may use at most 64 MiB of HBM per device.

v0:
```python
import math
import jax
import jax.numpy as jnp
from jax import lax
from jax.sharding import Mesh
from jax.sharding import PartitionSpec as P

HD = 128
EPSILON = 1e-06
HEAD_AXIS = "cx"
TOKEN_AXES = ("cz", "cc")
CTX_AXES = ("cx", "cz", "cc")


def head_norm(values):
    return values * lax.rsqrt(jnp.mean(values * values, axis=-1, keepdims=True) + EPSILON)


def to_head_groups(rows, groups):
    *lead, n, width = rows.shape
    split = rows.reshape(*lead, n, groups, width // groups)
    return jnp.moveaxis(split, -2, 0)


def per_device(
    perturbed_frame_activation,
    inbound_activation,
    section_block_indices,
    tile_arrival_permutation,
    adaptive_shifting,
    adaptive_scaling,
    tier_query_factor,
    tier_skip_coefficient,
    earlier_step_lookup_matrix,
    earlier_step_content_matrix,
):
    segment = lax.axis_index("segment")
    patch_count = tile_arrival_permutation.shape[0]
    rows = inbound_activation.shape[1]
    width = inbound_activation.shape[2]
    heads = width // HD
    groups = lax.axis_size(HEAD_AXIS)
    group_width = width // groups
    group_heads = heads // groups
    slot_count = earlier_step_lookup_matrix.shape[1]
    layers_here = section_block_indices[0]
    scale = 1.0 / math.sqrt(HD)

    def gather_head_group(kv_rows):
        parts = to_head_groups(kv_rows, groups)
        mine = lax.all_to_all(parts, HEAD_AXIS, 0, 0)
        mine = jnp.moveaxis(mine, 0, -3)
        mine = mine.reshape(*mine.shape[:-3], groups * rows, group_width)
        return lax.all_gather(mine, TOKEN_AXES, axis=mine.ndim - 2, tiled=True)

    other_patch = tile_arrival_permutation[jnp.mod(1 - segment, patch_count)]
    other_k = lax.dynamic_index_in_dim(
        earlier_step_lookup_matrix[0], other_patch, 1, keepdims=False
    )
    other_v = lax.dynamic_index_in_dim(
        earlier_step_content_matrix[0], other_patch, 1, keepdims=False
    )
    other_kv = gather_head_group(jnp.stack([other_k, other_v], axis=1))

    def layer(state, tier, far_kv):
        live = layers_here > tier
        x = state.astype(jnp.float32)
        hidden = (
            x
            * lax.rsqrt(jnp.mean(x * x, axis=-1, keepdims=True) + EPSILON)
            * (1.0 + adaptive_scaling[0, tier])
            + adaptive_shifting[0, tier]
        )
        query = head_norm(hidden.reshape(rows, heads, HD)).reshape(rows, width).astype(jnp.bfloat16)
        fresh_key = (
            head_norm((hidden * tier_query_factor[0, tier]).reshape(rows, heads, HD))
            .reshape(rows, width)
            .astype(jnp.bfloat16)
        )
        fresh_value = hidden.astype(jnp.bfloat16)
        packed = to_head_groups(jnp.stack([query, fresh_key, fresh_value]), groups)
        mine = lax.all_to_all(packed, HEAD_AXIS, 0, 0)
        local_q = mine[:, 0].reshape(groups * rows, group_heads, HD)
        near_kv = jnp.moveaxis(mine[:, 1:], 0, 1).reshape(2, groups * rows, group_width)
        near_kv = lax.all_gather(near_kv, TOKEN_AXES, axis=1, tiled=True)
        keys = jnp.concatenate([near_kv[0], far_kv[0]], axis=0)
        values = jnp.concatenate([near_kv[1], far_kv[1]], axis=0)
        key_count = keys.shape[0]
        scores = (
            jnp.einsum(
                "phd,nhd->phn",
                local_q,
                keys.reshape(key_count, group_heads, HD),
                preferred_element_type=jnp.float32,
            )
            * scale
        )
        weights = jnp.exp(scores)
        total = jnp.sum(weights, axis=-1)
        numerator = jnp.einsum(
            "phn,nhd->phd",
            weights.astype(jnp.bfloat16),
            values.reshape(key_count, group_heads, HD),
            preferred_element_type=jnp.float32,
        )
        attended = (numerator / total[..., None]).reshape(groups, rows, group_width)
        back = lax.all_to_all(attended, HEAD_AXIS, 0, 0)
        back = jnp.moveaxis(back, 0, 1).reshape(rows, width)
        new_state = (x + tier_skip_coefficient[0, tier] * back).astype(jnp.bfloat16)
        return (jnp.where(live, new_state, state), near_kv)

    outcomes = []
    state = jnp.where(
        segment == 0,
        lax.dynamic_index_in_dim(
            perturbed_frame_activation, tile_arrival_permutation[0], 0, keepdims=False
        ),
        inbound_activation[0],
    )
    first_turn_kv = []
    for tier in range(slot_count):
        state, near_kv = layer(state, tier, other_kv[tier])
        first_turn_kv.append(near_kv)
    outcomes.append(state)
    for turn in range(1, patch_count):
        count = lax.axis_size("segment")
        arrived = lax.ppermute(state, "segment", [(i, i + 1) for i in range(count - 1)])
        state = jnp.where(
            segment == 0,
            lax.dynamic_index_in_dim(
                perturbed_frame_activation, tile_arrival_permutation[turn], 0, keepdims=False
            ),
            arrived,
        )
        for tier in range(slot_count):
            state, _ = layer(state, tier, first_turn_kv[tier])
        outcomes.append(state)
    return jnp.stack(outcomes)[None]


def solution(mesh):
    segments, ctx = mesh.devices.shape
    heads_mesh = Mesh(mesh.devices.reshape(segments, 4, ctx // 8, 2), ("segment",) + CTX_AXES)
    return jax.shard_map(
        per_device,
        mesh=heads_mesh,
        in_specs=(
            P(None, CTX_AXES, None),
            P("segment", CTX_AXES, None),
            P("segment"),
            P(),
            P("segment", None, None),
            P("segment", None, None),
            P("segment", None, None),
            P("segment", None, None),
            P("segment", None, None, CTX_AXES, None),
            P("segment", None, None, CTX_AXES, None),
        ),
        out_specs=P("segment", None, CTX_AXES, None),
        check_vma=False,
    )
```

profile of v0, /device:TPU:32, one launch (start us, length us, event | category | flops | bytes accessed | tf_op | source)
XLA Modules:
  0.0 178.7 jit_solution(13781949084585847155)
XLA Ops:
  0.0 0.6 copy-done.8
  0.7 0.7 fusion.130
  3.6 0.6 copy-done.6
  4.5 0.6 maximum_bitcast_fusion.1
  5.1 4.4 %all-to-all-start = ((bf16[4,3,8,384]{3,2,1,0:T(8,128)(2,1)}), bf16[4,3,8,384]{3,2,1,0:T(8,128)(2,1)S(1)}, u32[]{:S(2)}, u32[]{:S(2)}) async-start(bf16[4,3,8,384]{3,2,1,0:T(8,128)(2,1)} %maximum_bitcast_fusion.1), calls=%async_computation | async-start | bytes 147456 | tf_op jit(solution)/shard_map/all_to_all | solution.py:82
  11.8 0.6 copy.78
  12.4 2.8 %all-to-all-done = bf16[4,3,8,384]{3,2,1,0:T(8,128)(2,1)S(1)} async-done(((bf16[4,3,8,384]{3,2,1,0:T(8,128)(2,1)}), bf16[4,3,8,384]{3,2,1,0:T(8,128)(2,1)S(1)}, u32[]{:S(2)}, u32[]{:S(2)}) %all-to-all-start) | async-done | bytes 73760 | tf_op jit(solution)/shard_map/all_to_all | solution.py:82
  15.2 3.3 %all-to-all-start.1 = ((bf16[4,2,2,8,384]{4,3,1,2,0:T(8,128)(2,1)}), bf16[4,2,2,8,384]{4,3,1,2,0:T(8,128)(2,1)S(1)}, u32[]{:S(2)}, u32[]{:S(2)}) async-start(bf16[4,2,2,8,384]{4,3,1,2,0:T(8,128)(2,1)} %copy.78), calls=%async_computation.1 | async-start | bytes 196608 | tf_op jit(solution)/shard_map/all_to_all | solution.py:51
  18.5 20.3 %all_gather.15 = bf16[2,256,384]{2,1,0:T(8,128)(2,1)S(1)} all-gather(bf16[2,32,384]{2,1,0:T(8,128)(2,1)S(1)} %copy_bitcast_fusion.4), channel_id=1, replica_groups=mesh['segment'=16,'cx'=4,'cz'=4,'cc'=2] {'cz','cc'}, dimensions={1}, use_global_device_ids=true | all-gather | bytes 442368 | tf_op jit(solution)/shard_map/all_gather | solution.py:85
  39.6 15.5 %all_gather.16 = bf16[2,2,256,384]{3,2,1,0:T(8,128)(2,1)S(1)} all-gather(bf16[2,2,32,384]{3,2,1,0:T(8,128)(2,1)S(1)} %bitcast.189), channel_id=1, replica_groups=mesh['segment'=16,'cx'=4,'cz'=4,'cc'=2] {'cz','cc'}, dimensions={2}, use_global_device_ids=true | all-gather | bytes 884736 | tf_op jit(solution)/shard_map/all_gather | solution.py:54
  56.4 0.6 reshape.603
  57.0 4.9 %all-to-all-start.2 = ((f32[4,8,384]{2,1,0:T(8,128)}), f32[4,8,384]{2,1,0:T(8,128)S(1)}, u32[]{:S(2)}, u32[]{:S(2)}) async-start(f32[4,8,384]{2,1,0:T(8,128)} %reshape.603), calls=%async_computation.2 | async-start | bytes 98304 | tf_op jit(solution)/shard_map/all_to_all | solution.py:107
  62.6 4.8 %all-to-all-done.2 = f32[4,8,384]{2,1,0:T(8,128)S(1)} async-done(((f32[4,8,384]{2,1,0:T(8,128)}), f32[4,8,384]{2,1,0:T(8,128)S(1)}, u32[]{:S(2)}, u32[]{:S(2)}) %all-to-all-start.2) | async-done | bytes 49184 | tf_op jit(solution)/shard_map/all_to_all | solution.py:107
  68.0 0.6 maximum_bitcast_fusion.2
  68.6 3.3 %all-to-all-start.3 = ((bf16[4,3,8,384]{3,2,1,0:T(8,128)(2,1)}), bf16[4,3,8,384]{3,2,1,0:T(8,128)(2,1)S(1)}, u32[]{:S(2)}, u32[]{:S(2)}) async-start(bf16[4,3,8,384]{3,2,1,0:T(8,128)(2,1)} %maximum_bitcast_fusion.2), calls=%async_computation.3 | async-start | bytes 147456 | tf_op jit(solution)/shard_map/all_to_all | solution.py:82
  72.5 5.0 %all-to-all-done.3 = bf16[4,3,8,384]{3,2,1,0:T(8,128)(2,1)S(1)} async-done(((bf16[4,3,8,384]{3,2,1,0:T(8,128)(2,1)}), bf16[4,3,8,384]{3,2,1,0:T(8,128)(2,1)S(1)}, u32[]{:S(2)}, u32[]{:S(2)}) %all-to-all-start.3) | async-done | bytes 73760 | tf_op jit(solution)/shard_map/all_to_all | solution.py:82
  77.5 14.9 %all_gather.17 = bf16[2,256,384]{2,1,0:T(8,128)(2,1)S(1)} all-gather(bf16[2,32,384]{2,1,0:T(8,128)(2,1)S(1)} %copy_bitcast_fusion.3), channel_id=1, replica_groups=mesh['segment'=16,'cx'=4,'cz'=4,'cc'=2] {'cz','cc'}, dimensions={1}, use_global_device_ids=true | all-gather | bytes 442368 | tf_op jit(solution)/shard_map/all_gather | solution.py:85
  93.7 0.6 reshape.608
  94.3 3.3 %all-to-all-start.4 = ((f32[4,8,384]{2,1,0:T(8,128)}), f32[4,8,384]{2,1,0:T(8,128)S(1)}, u32[]{:S(2)}, u32[]{:S(2)}) async-start(f32[4,8,384]{2,1,0:T(8,128)} %reshape.608), calls=%async_computation.4 | async-start | bytes 98304 | tf_op jit(solution)/shard_map/all_to_all | solution.py:107
  97.6 5.5 %all-to-all-done.4 = f32[4,8,384]{2,1,0:T(8,128)S(1)} async-done(((f32[4,8,384]{2,1,0:T(8,128)}), f32[4,8,384]{2,1,0:T(8,128)S(1)}, u32[]{:S(2)}, u32[]{:S(2)}) %all-to-all-start.4) | async-done | bytes 49184 | tf_op jit(solution)/shard_map/all_to_all | solution.py:107
  103.1 4.8 %collective-permute-start = (bf16[8,1536]{1,0:T(8,128)(2,1)S(1)}, bf16[8,1536]{1,0:T(8,128)(2,1)S(1)}, u32[]{:S(2)}, u32[]{:S(2)}) collective-permute-start(bf16[8,1536]{1,0:T(8,128)(2,1)S(1)} %fusion.104), channel_id=1, source_target_pairs={{0,32},{32,64},{64,96},{96,128},{128,160},{160,192},{192,224},{224... | collective-permute-start | bytes 73736 | tf_op jit(solution)/shard_map/ppermute | solution.py:127
  109.9 1.1 collective-permute-done
  111.5 8.0 %all_to_all.45 = bf16[4,3,8,384]{3,2,1,0:T(8,128)(2,1)S(1)} all-to-all(bf16[4,3,8,384]{3,2,1,0:T(8,128)(2,1)S(1)} %maximum_bitcast_fusion.3), channel_id=1, replica_groups=mesh['segment'=16,'cx'=4,'cz'=4,'cc'=2] {'cx'}, dimensions={0} | all-to-all | bytes 147456 | tf_op jit(solution)/shard_map/all_to_all | solution.py:82
  119.5 14.9 %all_gather.18 = bf16[2,256,384]{2,1,0:T(8,128)(2,1)S(1)} all-gather(bf16[2,32,384]{2,1,0:T(8,128)(2,1)S(1)} %copy_bitcast_fusion.2), channel_id=1, replica_groups=mesh['segment'=16,'cx'=4,'cz'=4,'cc'=2] {'cz','cc'}, dimensions={1}, use_global_device_ids=true | all-gather | bytes 442368 | tf_op jit(solution)/shard_map/all_gather | solution.py:85
  135.7 7.9 %all_to_all.46 = f32[4,8,384]{2,1,0:T(8,128)S(1)} all-to-all(f32[4,8,384]{2,1,0:T(8,128)S(1)} %reshape.612), channel_id=1, replica_groups=mesh['segment'=16,'cx'=4,'cz'=4,'cc'=2] {'cx'}, dimensions={0} | all-to-all | bytes 98304 | tf_op jit(solution)/shard_map/all_to_all | solution.py:107
  144.1 8.0 %all_to_all.47 = bf16[4,3,8,384]{3,2,1,0:T(8,128)(2,1)S(1)} all-to-all(bf16[4,3,8,384]{3,2,1,0:T(8,128)(2,1)S(1)} %maximum_bitcast_fusion.4), channel_id=1, replica_groups=mesh['segment'=16,'cx'=4,'cz'=4,'cc'=2] {'cx'}, dimensions={0} | all-to-all | bytes 147456 | tf_op jit(solution)/shard_map/all_to_all | solution.py:82
  152.1 15.2 %all_gather.19 = bf16[2,256,384]{2,1,0:T(8,128)(2,1)S(1)} all-gather(bf16[2,32,384]{2,1,0:T(8,128)(2,1)S(1)} %copy_bitcast_fusion.1), channel_id=1, replica_groups=mesh['segment'=16,'cx'=4,'cz'=4,'cc'=2] {'cz','cc'}, dimensions={1}, use_global_device_ids=true | all-gather | bytes 442368 | tf_op jit(solution)/shard_map/all_gather | solution.py:85
  168.0 0.3 fusion.134
  168.6 0.6 reshape.615
  169.3 3.3 %all-to-all-start.8 = ((f32[4,8,384]{2,1,0:T(8,128)}), f32[4,8,384]{2,1,0:T(8,128)S(1)}, u32[]{:S(2)}, u32[]{:S(2)}) async-start(f32[4,8,384]{2,1,0:T(8,128)} %reshape.615), calls=%async_computation.8 | async-start | bytes 98304 | tf_op jit(solution)/shard_map/all_to_all | solution.py:107
  172.6 5.5 %all-to-all-done.8 = f32[4,8,384]{2,1,0:T(8,128)S(1)} async-done(((f32[4,8,384]{2,1,0:T(8,128)}), f32[4,8,384]{2,1,0:T(8,128)S(1)}, u32[]{:S(2)}, u32[]{:S(2)}) %all-to-all-start.8) | async-done | bytes 49184 | tf_op jit(solution)/shard_map/all_to_all | solution.py:107
  178.1 0.6 maximum_bitcast_fusion.5
  (108 shorter events, 8.2 us)
Async XLA Ops:
  0.0 0.7 copy-start.8
  0.0 2.6 %copy-start.4 = (f32[1,2,1536]{2,1,0:T(2,128)S(1)}, f32[1,2,1536]{2,1,0:T(2,128)}, u32[]{:S(2)}) copy-start(f32[1,2,1536]{2,1,0:T(2,128)} %param.14) | copy-start | bytes 36868
  0.0 2.7 %copy-start.5 = (f32[1,2,1536]{2,1,0:T(2,128)S(1)}, f32[1,2,1536]{2,1,0:T(2,128)}, u32[]{:S(2)}) copy-start(f32[1,2,1536]{2,1,0:T(2,128)} %param.15) | copy-start | bytes 36868
  0.0 3.4 %copy-start = (bf16[2,8,1536]{2,1,0:T(8,128)(2,1)S(1)}, bf16[2,8,1536]{2,1,0:T(8,128)(2,1)}, u32[]{:S(2)}) copy-start(bf16[2,8,1536]{2,1,0:T(8,128)(2,1)} %param.10) | copy-start | bytes 147460
  2.6 0.8 copy-start.3
  3.4 0.7 copy-start.6
  4.5 7.2 %copy-start.2 = (bf16[1,2,2,8,1536]{4,3,2,1,0:T(8,128)(2,1)S(1)}, bf16[1,2,2,8,1536]{4,3,2,1,0:T(8,128)(2,1)}, u32[]{:S(2)}) copy-start(bf16[1,2,2,8,1536]{4,3,2,1,0:T(8,128)(2,1)} %param.18) | copy-start | bytes 294916
  5.1 6.5 %copy-start.1 = (bf16[1,2,2,8,1536]{4,3,2,1,0:T(8,128)(2,1)S(1)}, bf16[1,2,2,8,1536]{4,3,2,1,0:T(8,128)(2,1)}, u32[]{:S(2)}) copy-start(bf16[1,2,2,8,1536]{4,3,2,1,0:T(8,128)(2,1)} %param.19) | copy-start | bytes 294916
  5.1 10.1 %all-to-all-start = ((bf16[4,3,8,384]{3,2,1,0:T(8,128)(2,1)}), bf16[4,3,8,384]{3,2,1,0:T(8,128)(2,1)S(1)}, u32[]{:S(2)}, u32[]{:S(2)}) async-start(bf16[4,3,8,384]{3,2,1,0:T(8,128)(2,1)} %maximum_bitcast_fusion.1), calls=%async_computation | async-start | bytes 147456 | tf_op jit(solution)/shard_map/all_to_all | solution.py:82
  15.2 24.3 %all-to-all-start.1 = ((bf16[4,2,2,8,384]{4,3,1,2,0:T(8,128)(2,1)}), bf16[4,2,2,8,384]{4,3,1,2,0:T(8,128)(2,1)S(1)}, u32[]{:S(2)}, u32[]{:S(2)}) async-start(bf16[4,2,2,8,384]{4,3,1,2,0:T(8,128)(2,1)} %copy.78), calls=%async_computation.1 | async-start | bytes 196608 | tf_op jit(solution)/shard_map/all_to_all | solution.py:51
  57.0 4.9 %copy-start.7 = (f32[1,2,1536]{2,1,0:T(2,128)S(1)}, f32[1,2,1536]{2,1,0:T(2,128)}, u32[]{:S(2)}) copy-start(f32[1,2,1536]{2,1,0:T(2,128)} %param.17) | copy-start | bytes 36868
  57.0 10.4 %all-to-all-start.2 = ((f32[4,8,384]{2,1,0:T(8,128)}), f32[4,8,384]{2,1,0:T(8,128)S(1)}, u32[]{:S(2)}, u32[]{:S(2)}) async-start(f32[4,8,384]{2,1,0:T(8,128)} %reshape.603), calls=%async_computation.2 | async-start | bytes 98304 | tf_op jit(solution)/shard_map/all_to_all | solution.py:107
  68.6 8.9 %all-to-all-start.3 = ((bf16[4,3,8,384]{3,2,1,0:T(8,128)(2,1)}), bf16[4,3,8,384]{3,2,1,0:T(8,128)(2,1)S(1)}, u32[]{:S(2)}, u32[]{:S(2)}) async-start(bf16[4,3,8,384]{3,2,1,0:T(8,128)(2,1)} %maximum_bitcast_fusion.2), calls=%async_computation.3 | async-start | bytes 147456 | tf_op jit(solution)/shard_map/all_to_all | solution.py:82
  94.3 8.8 %all-to-all-start.4 = ((f32[4,8,384]{2,1,0:T(8,128)}), f32[4,8,384]{2,1,0:T(8,128)S(1)}, u32[]{:S(2)}, u32[]{:S(2)}) async-start(f32[4,8,384]{2,1,0:T(8,128)} %reshape.608), calls=%async_computation.4 | async-start | bytes 98304 | tf_op jit(solution)/shard_map/all_to_all | solution.py:107
  103.1 7.8 %collective-permute-start = (bf16[8,1536]{1,0:T(8,128)(2,1)S(1)}, bf16[8,1536]{1,0:T(8,128)(2,1)S(1)}, u32[]{:S(2)}, u32[]{:S(2)}) collective-permute-start(bf16[8,1536]{1,0:T(8,128)(2,1)S(1)} %fusion.104), channel_id=1, source_target_pairs={{0,32},{32,64},{64,96},{96,128},{128,160},{160,192},{192,224},{224... | collective-permute-start | bytes 73736 | tf_op jit(solution)/shard_map/ppermute | solution.py:127
  169.3 8.8 %all-to-all-start.8 = ((f32[4,8,384]{2,1,0:T(8,128)}), f32[4,8,384]{2,1,0:T(8,128)S(1)}, u32[]{:S(2)}, u32[]{:S(2)}) async-start(f32[4,8,384]{2,1,0:T(8,128)} %reshape.615), calls=%async_computation.8 | async-start | bytes 98304 | tf_op jit(solution)/shard_map/all_to_all | solution.py:107
where the time goes:
time: 180 us; the launch traced here: 179 us
  blocking collectives  105 us (58%)
  starting transfers between devices  27.2 us (15%)
  waiting for transfers between devices  24.7 us (14%)
  local copies, waits for them, and re-layouts  8.84 us (5%)
  between operations  7.15 us (4%)
  other arithmetic  3.88 us (2%)
  matrix products  2.12 us (1%)
    all_gather x4, blocking collectives, layer(): near_kv = lax.all_gather(near_kv, TOKEN_AXES, axis=1, tiled=True)  65.2 us
    all_to_all x2, blocking collectives, layer(): mine = lax.all_to_all(packed, HEAD_AXIS, 0, 0)  16.1 us
    all_to_all x3, waiting for transfers between devices, layer(): back = lax.all_to_all(attended, HEAD_AXIS, 0, 0)  15.8 us
    all_gather x1, blocking collectives, gather_head_group(): return lax.all_gather(mine, TOKEN_AXES, axis=mine.ndim - 2, tiled=True)  15.5 us
    all_to_all x3, starting transfers between devices, layer(): back = lax.all_to_all(attended, HEAD_AXIS, 0, 0)  11.4 us
    all_to_all x1, blocking collectives, layer(): back = lax.all_to_all(attended, HEAD_AXIS, 0, 0)  7.9 us
    all_to_all x2, waiting for transfers between devices, layer(): mine = lax.all_to_all(packed, HEAD_AXIS, 0, 0)  7.79 us
    all_to_all x2, starting transfers between devices, layer(): mine = lax.all_to_all(packed, HEAD_AXIS, 0, 0)  7.71 us
  transfers between devices with their start and end apart: 7, of which 6 were waited for; matrix products, arithmetic and copies ran while one was open for 1% of the time, Pallas kernels for 0%

commit v1 on v0

--- a/solution.py
+++ b/solution.py
@@ -82,7 +82,10 @@
         mine = lax.all_to_all(packed, HEAD_AXIS, 0, 0)
         local_q = mine[:, 0].reshape(groups * rows, group_heads, HD)
         near_kv = jnp.moveaxis(mine[:, 1:], 0, 1).reshape(2, groups * rows, group_width)
-        near_kv = lax.all_gather(near_kv, TOKEN_AXES, axis=1, tiled=True)
+        near_kv = jnp.concatenate(
+            lax.all_to_all(jnp.stack([near_kv] * lax.axis_size(TOKEN_AXES)), TOKEN_AXES, 0, 0),
+            axis=1,
+        )
         keys = jnp.concatenate([near_kv[0], far_kv[0]], axis=0)
         values = jnp.concatenate([near_kv[1], far_kv[1]], axis=0)
         key_count = keys.shape[0]

time: 180 us -> 193 us (1.072)
  the two profiles are of different devices: /device:TPU:32 before, /device:TPU:24 now
where the time goes in v1:
time: 193 us; the launch traced here: 192 us
  waiting for transfers between devices  70.3 us (36%)
  blocking collectives  56 us (29%)
  starting transfers between devices  43 us (22%)
  local copies, waits for them, and re-layouts  10.2 us (5%)
  between operations  7.21 us (4%)
  other arithmetic  3.26 us (2%)
  matrix products  2.09 us (1%)
    all_to_all x4, waiting for transfers between devices, layer(): lax.all_to_all(jnp.stack([near_kv] * lax.axis_size(TOKEN_AXES)), TOKEN_AX...  44.4 us
    all_to_all x3, blocking collectives, layer(): mine = lax.all_to_all(packed, HEAD_AXIS, 0, 0)  24.1 us
    all_gather x1, blocking collectives, gather_head_group(): return lax.all_gather(mine, TOKEN_AXES, axis=mine.ndim - 2, tiled=True)  24 us
    all_to_all x4, starting transfers between devices, layer(): lax.all_to_all(jnp.stack([near_kv] * lax.axis_size(TOKEN_AXES)), TOKEN_AX...  22.1 us
    all_to_all x3, waiting for transfers between devices, layer(): back = lax.all_to_all(attended, HEAD_AXIS, 0, 0)  15.8 us
    all_to_all x3, starting transfers between devices, layer(): back = lax.all_to_all(attended, HEAD_AXIS, 0, 0)  9.95 us
    all_to_all x1, blocking collectives, layer(): back = lax.all_to_all(attended, HEAD_AXIS, 0, 0)  7.9 us
    all_to_all x1, waiting for transfers between devices, gather_head_group(): mine = lax.all_to_all(parts, HEAD_AXIS, 0, 0)  5.75 us
  transfers between devices with their start and end apart: 10, of which 9 were waited for; matrix products, arithmetic and copies ran while one was open for 1% of the time, Pallas kernels for 0%

profile of v1, /device:TPU:24, one launch (start us, length us, event | category | flops | bytes accessed | tf_op | source)
XLA Modules:
  0.0 192.1 jit_solution(8899086676299660059)
XLA Ops:
  0.7 0.7 fusion.130
  5.1 4.4 %all-to-all-start = ((bf16[4,3,8,384]{3,2,1,0:T(8,128)(2,1)}), bf16[4,3,8,384]{3,2,1,0:T(8,128)(2,1)S(1)}, u32[]{:S(2)}, u32[]{:S(2)}) async-start(bf16[4,3,8,384]{3,2,1,0:T(8,128)(2,1)} %maximum_bitcast_fusion.1), calls=%async_computation | async-start | bytes 147456 | tf_op jit(solution)/shard_map/all_to_all | solution.py:82
  12.4 2.8 %all-to-all-done = bf16[4,3,8,384]{3,2,1,0:T(8,128)(2,1)S(1)} async-done(((bf16[4,3,8,384]{3,2,1,0:T(8,128)(2,1)}), bf16[4,3,8,384]{3,2,1,0:T(8,128)(2,1)S(1)}, u32[]{:S(2)}, u32[]{:S(2)}) %all-to-all-start) | async-done | bytes 73760 | tf_op jit(solution)/shard_map/all_to_all | solution.py:82
  15.2 3.3 %all-to-all-start.2 = ((bf16[4,2,2,8,384]{4,3,1,2,0:T(8,128)(2,1)}), bf16[4,2,2,8,384]{4,3,1,2,0:T(8,128)(2,1)S(1)}, u32[]{:S(2)}, u32[]{:S(2)}) async-start(bf16[4,2,2,8,384]{4,3,1,2,0:T(8,128)(2,1)} %copy.95), calls=%async_computation.2 | async-start | bytes 196608 | tf_op jit(solution)/shard_map/all_to_all | solution.py:51
  18.5 5.8 %all-to-all-done.2 = bf16[4,2,2,8,384]{4,3,1,2,0:T(8,128)(2,1)S(1)} async-done(((bf16[4,2,2,8,384]{4,3,1,2,0:T(8,128)(2,1)}), bf16[4,2,2,8,384]{4,3,1,2,0:T(8,128)(2,1)S(1)}, u32[]{:S(2)}, u32[]{:S(2)}) %all-to-all-start.2) | async-done | bytes 98336 | tf_op jit(solution)/shard_map/all_to_all | solution.py:51
  24.3 0.8 stack.80
  25.1 10.3 %all-to-all-start.1 = ((bf16[8,2,32,384]{3,2,1,0:T(8,128)(2,1)}), bf16[8,2,32,384]{3,2,1,0:T(8,128)(2,1)S(1)}, u32[]{:S(2)}, u32[]{:S(2)}) async-start(bf16[8,2,32,384]{3,2,1,0:T(8,128)(2,1)} %stack.80), calls=%async_computation.1 | async-start | bytes 786432 | tf_op jit(solution)/shard_map/all_to_all | solution.py:86
  35.4 24.0 %all_gather.3 = bf16[2,2,256,384]{3,2,1,0:T(8,128)(2,1)S(1)} all-gather(bf16[2,2,32,384]{3,2,1,0:T(8,128)(2,1)S(1)} %bitcast.213), channel_id=1, replica_groups=mesh['segment'=16,'cx'=4,'cz'=4,'cc'=2] {'cz','cc'}, dimensions={2}, use_global_device_ids=true | all-gather | bytes 884736 | tf_op jit(solution)/shard_map/all_gather | solution.py:54
  61.0 0.6 reshape.631
  61.6 3.4 %all-to-all-start.3 = ((f32[4,8,384]{2,1,0:T(8,128)}), f32[4,8,384]{2,1,0:T(8,128)S(1)}, u32[]{:S(2)}, u32[]{:S(2)}) async-start(f32[4,8,384]{2,1,0:T(8,128)} %reshape.631), calls=%async_computation.3 | async-start | bytes 98304 | tf_op jit(solution)/shard_map/all_to_all | solution.py:110
  65.7 4.8 %all-to-all-done.3 = f32[4,8,384]{2,1,0:T(8,128)S(1)} async-done(((f32[4,8,384]{2,1,0:T(8,128)}), f32[4,8,384]{2,1,0:T(8,128)S(1)}, u32[]{:S(2)}, u32[]{:S(2)}) %all-to-all-start.3) | async-done | bytes 49184 | tf_op jit(solution)/shard_map/all_to_all | solution.py:110
  71.1 8.0 %all_to_all.65 = bf16[4,3,8,384]{3,2,1,0:T(8,128)(2,1)S(1)} all-to-all(bf16[4,3,8,384]{3,2,1,0:T(8,128)(2,1)S(1)} %maximum_bitcast_fusion.2), channel_id=1, replica_groups=mesh['segment'=16,'cx'=4,'cz'=4,'cc'=2] {'cx'}, dimensions={0} | all-to-all | bytes 147456 | tf_op jit(solution)/shard_map/all_to_all | solution.py:82
  79.1 0.8 stack.88
  79.9 4.9 %all-to-all-start.5 = ((bf16[8,2,32,384]{3,2,1,0:T(8,128)(2,1)}), bf16[8,2,32,384]{3,2,1,0:T(8,128)(2,1)S(1)}, u32[]{:S(2)}, u32[]{:S(2)}) async-start(bf16[8,2,32,384]{3,2,1,0:T(8,128)(2,1)} %stack.88), calls=%async_computation.5 | async-start | bytes 786432 | tf_op jit(solution)/shard_map/all_to_all | solution.py:86
  85.5 14.1 %all-to-all-done.5 = bf16[8,2,32,384]{3,2,1,0:T(8,128)(2,1)S(1)} async-done(((bf16[8,2,32,384]{3,2,1,0:T(8,128)(2,1)}), bf16[8,2,32,384]{3,2,1,0:T(8,128)(2,1)S(1)}, u32[]{:S(2)}, u32[]{:S(2)}) %all-to-all-start.5) | async-done | bytes 393248 | tf_op jit(solution)/shard_map/all_to_all | solution.py:86
  100.5 0.6 reshape.636
  101.1 3.3 %all-to-all-start.6 = ((f32[4,8,384]{2,1,0:T(8,128)}), f32[4,8,384]{2,1,0:T(8,128)S(1)}, u32[]{:S(2)}, u32[]{:S(2)}) async-start(f32[4,8,384]{2,1,0:T(8,128)} %reshape.636), calls=%async_computation.6 | async-start | bytes 98304 | tf_op jit(solution)/shard_map/all_to_all | solution.py:110
  104.4 5.5 %all-to-all-done.6 = f32[4,8,384]{2,1,0:T(8,128)S(1)} async-done(((f32[4,8,384]{2,1,0:T(8,128)}), f32[4,8,384]{2,1,0:T(8,128)S(1)}, u32[]{:S(2)}, u32[]{:S(2)}) %all-to-all-start.6) | async-done | bytes 49184 | tf_op jit(solution)/shard_map/all_to_all | solution.py:110
  109.9 3.2 %collective-permute-start = (bf16[8,1536]{1,0:T(8,128)(2,1)S(1)}, bf16[8,1536]{1,0:T(8,128)(2,1)S(1)}, u32[]{:S(2)}, u32[]{:S(2)}) collective-permute-start(bf16[8,1536]{1,0:T(8,128)(2,1)S(1)} %fusion.104), channel_id=1, source_target_pairs={{0,32},{32,64},{64,96},{96,128},{128,160},{160,192},{192,224},{224... | collective-permute-start | bytes 73736 | tf_op jit(solution)/shard_map/ppermute | solution.py:130
  115.0 1.5 collective-permute-done
  117.0 8.0 %all_to_all.66 = bf16[4,3,8,384]{3,2,1,0:T(8,128)(2,1)S(1)} all-to-all(bf16[4,3,8,384]{3,2,1,0:T(8,128)(2,1)S(1)} %maximum_bitcast_fusion.3), channel_id=1, replica_groups=mesh['segment'=16,'cx'=4,'cz'=4,'cc'=2] {'cx'}, dimensions={0} | all-to-all | bytes 147456 | tf_op jit(solution)/shard_map/all_to_all | solution.py:82
  125.1 0.8 stack.93
  125.8 3.5 %all-to-all-start.8 = ((bf16[8,2,32,384]{3,2,1,0:T(8,128)(2,1)}), bf16[8,2,32,384]{3,2,1,0:T(8,128)(2,1)S(1)}, u32[]{:S(2)}, u32[]{:S(2)}) async-start(bf16[8,2,32,384]{3,2,1,0:T(8,128)(2,1)} %stack.93), calls=%async_computation.8 | async-start | bytes 786432 | tf_op jit(solution)/shard_map/all_to_all | solution.py:86
  129.3 15.4 %all-to-all-done.8 = bf16[8,2,32,384]{3,2,1,0:T(8,128)(2,1)S(1)} async-done(((bf16[8,2,32,384]{3,2,1,0:T(8,128)(2,1)}), bf16[8,2,32,384]{3,2,1,0:T(8,128)(2,1)S(1)}, u32[]{:S(2)}, u32[]{:S(2)}) %all-to-all-start.8) | async-done | bytes 393248 | tf_op jit(solution)/shard_map/all_to_all | solution.py:86
  145.6 7.9 %all_to_all.67 = f32[4,8,384]{2,1,0:T(8,128)S(1)} all-to-all(f32[4,8,384]{2,1,0:T(8,128)S(1)} %reshape.640), channel_id=1, replica_groups=mesh['segment'=16,'cx'=4,'cz'=4,'cc'=2] {'cx'}, dimensions={0} | all-to-all | bytes 98304 | tf_op jit(solution)/shard_map/all_to_all | solution.py:110
  154.0 8.0 %all_to_all.68 = bf16[4,3,8,384]{3,2,1,0:T(8,128)(2,1)S(1)} all-to-all(bf16[4,3,8,384]{3,2,1,0:T(8,128)(2,1)S(1)} %maximum_bitcast_fusion.4), channel_id=1, replica_groups=mesh['segment'=16,'cx'=4,'cz'=4,'cc'=2] {'cx'}, dimensions={0} | all-to-all | bytes 147456 | tf_op jit(solution)/shard_map/all_to_all | solution.py:82
  162.1 0.8 stack.98
  162.8 3.5 %all-to-all-start.11 = ((bf16[8,2,32,384]{3,2,1,0:T(8,128)(2,1)}), bf16[8,2,32,384]{3,2,1,0:T(8,128)(2,1)S(1)}, u32[]{:S(2)}, u32[]{:S(2)}) async-start(bf16[8,2,32,384]{3,2,1,0:T(8,128)(2,1)} %stack.98), calls=%async_computation.11 | async-start | bytes 786432 | tf_op jit(solution)/shard_map/all_to_all | solution.py:86
  166.3 14.8 %all-to-all-done.11 = bf16[8,2,32,384]{3,2,1,0:T(8,128)(2,1)S(1)} async-done(((bf16[8,2,32,384]{3,2,1,0:T(8,128)(2,1)}), bf16[8,2,32,384]{3,2,1,0:T(8,128)(2,1)S(1)}, u32[]{:S(2)}, u32[]{:S(2)}) %all-to-all-start.11) | async-done | bytes 393248 | tf_op jit(solution)/shard_map/all_to_all | solution.py:86
  182.0 0.6 reshape.643
  182.6 3.3 %all-to-all-start.12 = ((f32[4,8,384]{2,1,0:T(8,128)}), f32[4,8,384]{2,1,0:T(8,128)S(1)}, u32[]{:S(2)}, u32[]{:S(2)}) async-start(f32[4,8,384]{2,1,0:T(8,128)} %reshape.643), calls=%async_computation.12 | async-start | bytes 98304 | tf_op jit(solution)/shard_map/all_to_all | solution.py:110
  186.0 5.5 %all-to-all-done.12 = f32[4,8,384]{2,1,0:T(8,128)S(1)} async-done(((f32[4,8,384]{2,1,0:T(8,128)}), f32[4,8,384]{2,1,0:T(8,128)S(1)}, u32[]{:S(2)}, u32[]{:S(2)}) %all-to-all-start.12) | async-done | bytes 49184 | tf_op jit(solution)/shard_map/all_to_all | solution.py:110
  (115 shorter events, 9.9 us)
Async XLA Ops:
  0.0 0.7 copy-start.8
  0.0 2.6 %copy-start.4 = (f32[1,2,1536]{2,1,0:T(2,128)S(1)}, f32[1,2,1536]{2,1,0:T(2,128)}, u32[]{:S(2)}) copy-start(f32[1,2,1536]{2,1,0:T(2,128)} %param.14) | copy-start | bytes 36868
  0.0 2.7 %copy-start.5 = (f32[1,2,1536]{2,1,0:T(2,128)S(1)}, f32[1,2,1536]{2,1,0:T(2,128)}, u32[]{:S(2)}) copy-start(f32[1,2,1536]{2,1,0:T(2,128)} %param.15) | copy-start | bytes 36868
  0.0 3.4 %copy-start = (bf16[2,8,1536]{2,1,0:T(8,128)(2,1)S(1)}, bf16[2,8,1536]{2,1,0:T(8,128)(2,1)}, u32[]{:S(2)}) copy-start(bf16[2,8,1536]{2,1,0:T(8,128)(2,1)} %param.10) | copy-start | bytes 147460
  2.6 0.8 copy-start.3
  3.4 0.7 copy-start.6
  4.5 7.2 %copy-start.2 = (bf16[1,2,2,8,1536]{4,3,2,1,0:T(8,128)(2,1)S(1)}, bf16[1,2,2,8,1536]{4,3,2,1,0:T(8,128)(2,1)}, u32[]{:S(2)}) copy-start(bf16[1,2,2,8,1536]{4,3,2,1,0:T(8,128)(2,1)} %param.18) | copy-start | bytes 294916
  5.1 6.5 %copy-start.1 = (bf16[1,2,2,8,1536]{4,3,2,1,0:T(8,128)(2,1)S(1)}, bf16[1,2,2,8,1536]{4,3,2,1,0:T(8,128)(2,1)}, u32[]{:S(2)}) copy-start(bf16[1,2,2,8,1536]{4,3,2,1,0:T(8,128)(2,1)} %param.19) | copy-start | bytes 294916
  5.1 10.1 %all-to-all-start = ((bf16[4,3,8,384]{3,2,1,0:T(8,128)(2,1)}), bf16[4,3,8,384]{3,2,1,0:T(8,128)(2,1)S(1)}, u32[]{:S(2)}, u32[]{:S(2)}) async-start(bf16[4,3,8,384]{3,2,1,0:T(8,128)(2,1)} %maximum_bitcast_fusion.1), calls=%async_computation | async-start | bytes 147456 | tf_op jit(solution)/shard_map/all_to_all | solution.py:82
  15.2 9.1 %all-to-all-start.2 = ((bf16[4,2,2,8,384]{4,3,1,2,0:T(8,128)(2,1)}), bf16[4,2,2,8,384]{4,3,1,2,0:T(8,128)(2,1)S(1)}, u32[]{:S(2)}, u32[]{:S(2)}) async-start(bf16[4,2,2,8,384]{4,3,1,2,0:T(8,128)(2,1)} %copy.95), calls=%async_computation.2 | async-start | bytes 196608 | tf_op jit(solution)/shard_map/all_to_all | solution.py:51
  25.1 35.1 %all-to-all-start.1 = ((bf16[8,2,32,384]{3,2,1,0:T(8,128)(2,1)}), bf16[8,2,32,384]{3,2,1,0:T(8,128)(2,1)S(1)}, u32[]{:S(2)}, u32[]{:S(2)}) async-start(bf16[8,2,32,384]{3,2,1,0:T(8,128)(2,1)} %stack.80), calls=%async_computation.1 | async-start | bytes 786432 | tf_op jit(solution)/shard_map/all_to_all | solution.py:86
  61.6 3.4 %copy-start.7 = (f32[1,2,1536]{2,1,0:T(2,128)S(1)}, f32[1,2,1536]{2,1,0:T(2,128)}, u32[]{:S(2)}) copy-start(f32[1,2,1536]{2,1,0:T(2,128)} %param.17) | copy-start | bytes 36868
  61.6 8.9 %all-to-all-start.3 = ((f32[4,8,384]{2,1,0:T(8,128)}), f32[4,8,384]{2,1,0:T(8,128)S(1)}, u32[]{:S(2)}, u32[]{:S(2)}) async-start(f32[4,8,384]{2,1,0:T(8,128)} %reshape.631), calls=%async_computation.3 | async-start | bytes 98304 | tf_op jit(solution)/shard_map/all_to_all | solution.py:110
  79.9 19.7 %all-to-all-start.5 = ((bf16[8,2,32,384]{3,2,1,0:T(8,128)(2,1)}), bf16[8,2,32,384]{3,2,1,0:T(8,128)(2,1)S(1)}, u32[]{:S(2)}, u32[]{:S(2)}) async-start(bf16[8,2,32,384]{3,2,1,0:T(8,128)(2,1)} %stack.88), calls=%async_computation.5 | async-start | bytes 786432 | tf_op jit(solution)/shard_map/all_to_all | solution.py:86
  101.1 8.8 %all-to-all-start.6 = ((f32[4,8,384]{2,1,0:T(8,128)}), f32[4,8,384]{2,1,0:T(8,128)S(1)}, u32[]{:S(2)}, u32[]{:S(2)}) async-start(f32[4,8,384]{2,1,0:T(8,128)} %reshape.636), calls=%async_computation.6 | async-start | bytes 98304 | tf_op jit(solution)/shard_map/all_to_all | solution.py:110
  109.9 6.6 %collective-permute-start = (bf16[8,1536]{1,0:T(8,128)(2,1)S(1)}, bf16[8,1536]{1,0:T(8,128)(2,1)S(1)}, u32[]{:S(2)}, u32[]{:S(2)}) collective-permute-start(bf16[8,1536]{1,0:T(8,128)(2,1)S(1)} %fusion.104), channel_id=1, source_target_pairs={{0,32},{32,64},{64,96},{96,128},{128,160},{160,192},{192,224},{224... | collective-permute-start | bytes 73736 | tf_op jit(solution)/shard_map/ppermute | solution.py:130
  125.8 18.9 %all-to-all-start.8 = ((bf16[8,2,32,384]{3,2,1,0:T(8,128)(2,1)}), bf16[8,2,32,384]{3,2,1,0:T(8,128)(2,1)S(1)}, u32[]{:S(2)}, u32[]{:S(2)}) async-start(bf16[8,2,32,384]{3,2,1,0:T(8,128)(2,1)} %stack.93), calls=%async_computation.8 | async-start | bytes 786432 | tf_op jit(solution)/shard_map/all_to_all | solution.py:86
  162.8 18.3 %all-to-all-start.11 = ((bf16[8,2,32,384]{3,2,1,0:T(8,128)(2,1)}), bf16[8,2,32,384]{3,2,1,0:T(8,128)(2,1)S(1)}, u32[]{:S(2)}, u32[]{:S(2)}) async-start(bf16[8,2,32,384]{3,2,1,0:T(8,128)(2,1)} %stack.98), calls=%async_computation.11 | async-start | bytes 786432 | tf_op jit(solution)/shard_map/all_to_all | solution.py:86
  182.6 8.8 %all-to-all-start.12 = ((f32[4,8,384]{2,1,0:T(8,128)}), f32[4,8,384]{2,1,0:T(8,128)S(1)}, u32[]{:S(2)}, u32[]{:S(2)}) async-start(f32[4,8,384]{2,1,0:T(8,128)} %reshape.643), calls=%async_computation.12 | async-start | bytes 98304 | tf_op jit(solution)/shard_map/all_to_all | solution.py:110
